TPU v7x, 32 devices: a whole 2x2x4 slice. The times are simulated.
32 devices in a mesh: grp: 4 (over y, x), dev: 8 (over z, core).
Axes of the slice: x: 2, y: 2, z: 4, core: 2. Of those that a mesh axis runs over, the one named last changes fastest.
Arguments:
- panel_nodes: float32 [3, 262144], P(None, ('grp', 'dev')), may hold values from -1.6 to 1.6, as said below
- density: float32 [262144], P(('grp', 'dev')), may hold values from -6 to 6
- crevice_routes: int32 [16384, 2], P(('grp', 'dev')), may hold values from 0 to 31, all different within a row; in each aligned block of 512 rows (0 to 511, 512 to 1023, ...) at most 64 rows name the same one
- crevice_centre: int32 [16384, 2], P(('grp', 'dev')), may hold values from 0 to 511
- centres: float32 [3, 16384], P(None, ('grp', 'dev')), may hold values from -0.3 to 0.3, as said below
- targets: float32 [3, 262144], P(None, ('grp', 'dev')), may hold values from -0.8 to 0.8, as said below
- centre_home: int32 [16384, 1], P(('grp', 'dev')), may hold values from 0 to 31; in each aligned block of 512 rows (0 to 511, 512 to 1023, ...) at most 32 rows name the same one
- upsample: float32 [64, 16], replicated, may hold values from 0 to 1, as said below
- fine_weights: float32 [64], replicated, may hold values from 0.005 to 0.05
Outputs:
- returned: float32 [524288], P(('grp', 'dev'))
Inputs may be any that keep to these rules, and one draw needn't show every extreme that they name: `crevice_routes`: each device's 512 panels name at most 64 (panel, route) pairs for any one owner device, and some owner reaches 64 in every draw; the 2 owners of one panel differ. `centre_home`: among the 512 centres of one device at most 32 have the same home, and that bound is reached in every draw; entries of returned with no centre are zero. `panel_nodes`: every point in the convex hull of one panel's nodes lies at distance 0.9 or more from the anchor; every panel node lies within 1.6 of the anchor. `centres`: every centre lies within 0.3 of the anchor. `targets`: each target node lies at distance 0.3 to 0.5 from its centre. `upsample`: entries are positive and each row sums to one.
All inputs are finite; a program needn't handle non-finite values.
Results may differ from a plain program's by a relative error of at most 0.0003.
Values sent between devices are 32-bit elements; how exact they have to be, the bound alone decides.
No kernel may reach another device: no remote copies, remote signals or barrier semaphores. Data moves between devices by JAX's collectives and lax.ppermute only.
A program may use at most 64 MiB of HBM per device.

v0:
```python
import jax
import jax.numpy as jnp
from jax import lax
from jax.sharding import PartitionSpec as P

ORDER = 8
HI = lax.Precision.HIGHEST


def route_rank(destination, count):
    rows = destination.shape[0]
    onehot = (destination[:, None] == jnp.arange(count, dtype=jnp.int32)[None, :]).astype(
        jnp.bfloat16
    )
    lower = (jnp.arange(rows)[:, None] > jnp.arange(rows)[None, :]).astype(jnp.bfloat16)
    before = jnp.dot(lower, onehot, preferred_element_type=jnp.float32)
    return jnp.sum(before * onehot.astype(jnp.float32), axis=1).astype(jnp.int32)


def expansion_terms(fine, strength, centre_pos, rel_targets):
    src = fine - centre_pos[:, None, :]
    rs2 = jnp.sum(src * src, axis=0)
    rt2 = jnp.sum(rel_targets * rel_targets, axis=0)
    inv_rs2 = 1.0 / rs2
    scale = strength * lax.rsqrt(rs2)
    inner = jnp.sum(src[:, :, None, :] * rel_targets[:, None, :, :], axis=0)
    w = inner * inv_rs2[:, None, :]
    rho2 = rt2[None, :, :] * inv_rs2[:, None, :]
    p_prev = jnp.ones_like(w)
    p_now = w
    total = 1.0 + w
    for level in range(1, ORDER):
        p_next = (2 * level + 1) / (level + 1) * w * p_now - level / (level + 1) * rho2 * p_prev
        total = total + p_next
        p_prev, p_now = (p_now, p_next)
    return jnp.sum(scale[:, None, :] * total, axis=0)


def per_device(
    panel_nodes,
    density,
    crevice_routes,
    crevice_centre,
    centres,
    targets,
    centre_home,
    upsample,
    fine_weights,
):
    devices = lax.axis_size(("grp", "dev"))
    panels = crevice_routes.shape[0]
    fanout = crevice_routes.shape[1]
    centre_count = centres.shape[1]
    capacity = max(2, 2 * panels * fanout // devices)
    capacity_back = max(2, 2 * centre_count // devices)
    fine_count, nodes = upsample.shape
    pairs = panels * fanout
    slots = devices * capacity
    coarse = jnp.concatenate(
        [
            panel_nodes.reshape(3, panels, nodes).transpose(0, 2, 1).reshape(3 * nodes, panels),
            density.reshape(panels, nodes).T,
        ],
        axis=0,
    )
    coarse_pairs = jnp.repeat(coarse, fanout, axis=1)
    ids_pairs = (crevice_centre.reshape(1, pairs) + 1).astype(jnp.float32)
    payload = jnp.concatenate([coarse_pairs, ids_pairs], axis=0)
    destination = crevice_routes.reshape(-1)
    slot_index = destination * capacity + route_rank(destination, devices)
    place = (slot_index[:, None] == jnp.arange(slots, dtype=jnp.int32)[None, :]).astype(jnp.float32)
    outgoing = jnp.dot(payload, place, precision=HI)
    incoming = lax.all_to_all(outgoing, ("grp", "dev"), split_axis=1, concat_axis=1, tiled=True)
    ids = jnp.round(incoming[4 * nodes]).astype(jnp.int32) - 1
    valid = ids >= 0
    pick = (ids[:, None] == jnp.arange(centre_count, dtype=jnp.int32)[None, :]).astype(jnp.float32)
    centre_pos = centres
    rel = targets.reshape(3, centre_count, nodes) - centre_pos[:, :, None]
    centre_data = jnp.concatenate(
        [centre_pos, rel.transpose(0, 2, 1).reshape(3 * nodes, centre_count)], axis=0
    )
    gathered = lax.dot_general(centre_data, pick, (((1,), (1,)), ((), ())), precision=HI)
    slot_centre = gathered[:3]
    slot_targets = gathered[3:].reshape(3, nodes, slots)
    coarse_in = incoming[: 4 * nodes].reshape(4, nodes, slots)
    upper = jnp.einsum("jn,cns->cjs", upsample, coarse_in, precision=HI)
    strength = upper[3] * fine_weights[:, None]
    terms = expansion_terms(upper[:3], strength, slot_centre, slot_targets)
    terms = jnp.where(valid[None, :], terms, 0.0)
    potential = jnp.dot(terms, pick, precision=HI)
    home = centre_home.reshape(-1)
    back_index = home * capacity_back + route_rank(home, devices)
    back_place = (
        back_index[None, :] == jnp.arange(devices * capacity_back, dtype=jnp.int32)[:, None]
    ).astype(jnp.float32)
    sending = lax.dot_general(back_place, potential, (((1,), (1,)), ((), ())), precision=HI)
    sending = sending.reshape(devices, capacity_back * nodes)
    returned = lax.all_to_all(sending, ("grp", "dev"), split_axis=0, concat_axis=0, tiled=True)
    return returned.reshape(-1)


def solution(mesh):
    placed = (
        P(None, ("grp", "dev")),
        P(("grp", "dev")),
        P(("grp", "dev"), None),
        P(("grp", "dev"), None),
        P(None, ("grp", "dev")),
        P(None, ("grp", "dev")),
        P(("grp", "dev"), None),
        P(),
        P(),
    )
    return jax.shard_map(
        per_device, mesh=mesh, in_specs=placed, out_specs=P(("grp", "dev")), check_vma=False
    )
```

profile of v0, /device:TPU:0, one launch (start us, length us, event | category | flops | bytes accessed | tf_op | source)
XLA Modules:
  0.0 91.0 jit_solution(11559862471947307797)
XLA Ops:
  0.0 0.7 add_convert_fusion
  1.1 0.9 reshape.130
  2.0 0.8 copy.45
  3.1 0.5 fusion.26
  3.6 1.2 %reshape.128 = f32[3,512,16]{2,1,0:T(8,128)S(1)} reshape(f32[3,8192]{1,0:T(4,128)} %param.9) | data formatting | bytes 196608 | tf_op jit(solution)/shard_map/reshape | solution.py:61
  4.8 0.2 copy.40
  5.4 8.0 %fusion.17 = f32[65,2048]{0,1:T(8,128)} fusion(s32[1024]{0:T(1024)S(1)} %convert_add_fusion, f32[1,1024]{0,1:T(8,128)S(1)} %convert_element_type.66, f32[64,1024]{0,1:T(8,128)S(1)} %bitcast.29), kind=kOutput, calls=%fused_computation.27 | convolution fusion | flops 1637942272 | bytes 802816 | tf_op jit(solution)/shard_map/all_to_all | solution.py:73
  13.4 7.5 %all-to-all-start = ((f32[65,32,64]{0,2,1:T(8,128)}), f32[65,32,64]{0,2,1:T(8,128)S(1)}, u32[]{:S(2)}, u32[]{:S(2)}) async-start(f32[65,32,64]{0,2,1:T(8,128)} %bitcast.5), calls=%async_computation | async-start | bytes 2097152 | tf_op jit(solution)/shard_map/all_to_all | solution.py:73
  20.9 0.3 reshape.134
  21.2 0.3 subtract_bitcast_fusion
  21.7 0.3 fusion.27
  22.0 26.3 %all-to-all-done = f32[65,32,64]{0,2,1:T(8,128)S(1)} async-done(((f32[65,32,64]{0,2,1:T(8,128)}), f32[65,32,64]{0,2,1:T(8,128)S(1)}, u32[]{:S(2)}, u32[]{:S(2)}) %all-to-all-start) | async-done | bytes 532512 | tf_op jit(solution)/shard_map/all_to_all | solution.py:73
  48.3 0.9 fusion.30
  49.3 2.2 %fusion.19 = f32[51,2048]{1,0:T(8,128)S(1)} fusion(s32[2048]{0:T(1024)S(1)} %sub.44, f32[48,512]{1,0:T(8,128)S(1)} %bitcast.33, f32[3,512]{1,0:T(4,128)S(1)} %copy-done.2), kind=kOutput, calls=%fused_computation.30 | convolution fusion | flops 642803200 | bytes 530432 | tf_op jit(solution)/shard_map/dot_general | solution.py:82
  51.6 0.9 %copy.47 = f32[64,32,64]{2,1,0:T(8,128)S(1)} copy(f32[64,32,64]{0,2,1:T(8,128)S(1)} %bitcast.25) | data formatting | bytes 1048576 | tf_op jit(solution)/shard_map/slice | solution.py:85
  52.5 0.4 reshape.133
  52.9 1.9 %convolution_bitcast_fusion = f32[4,64,2048]{2,1,0:T(8,128)S(1)} fusion(f32[4,16,2048]{2,1,0:T(8,128)S(1)} %reshape.133, f32[64,16]{0,1:T(8,128)S(1)} %copy-done), kind=kOutput, calls=%fused_computation.34 | convolution fusion | flops 100663296 | bytes 2625536 | tf_op jit(solution)/shard_map/jn,cns->cjs/dot_general | solution.py:86
  54.8 1.5 %multiply_reduce_fusion.1 = (f32[64,2048]{1,0:T(8,128)S(1)}, f32[3,64,2048]{2,1,0:T(8,128)}) fusion(f32[3,2048]{1,0:T(4,128)S(1)} %slice.30, f32[4,64,2048]{2,1,0:T(8,128)S(1)} %convolution_bitcast_fusion), kind=kLoop, calls=%fused_computation.40 | loop fusion | flops 1048576 | bytes 3694592 | tf_op jit(solution)/shard_map/reduce_sum | solution.py:22
  56.3 7.7 %multiply_reduce_fusion = f32[64,16,2048]{2,1,0:T(8,128)} fusion(f32[3,16,2048]{2,1,0:T(8,128)S(1)} %bitcast.27, f32[3,64,2048]{2,1,0:T(8,128)} %get-tuple-element.6), kind=kLoop, calls=%fused_computation.7 | loop fusion | flops 10485760 | bytes 10354688 | tf_op jit(solution)/shard_map/reduce_sum | solution.py:26
  64.1 14.1 %fusion.15 = f32[16,2048]{1,0:T(8,128)S(1)} fusion(f32[64,16,2048]{2,1,0:T(8,128)} %multiply_reduce_fusion, f32[16,2048]{1,0:T(8,128)S(1)} %multiply_reduce_fusion.2, f32[64,2048]{1,0:T(8,128)S(1)} %get-tuple-element.8, f32[64,2048]{1,0:T(8,128)S(1)} %get-tuple-element.7), kind=kLoop, calls=%fused_computation.24 | loop fusion | flops 96436224 | bytes 9699328 | tf_op jit(solution)/shard_map/reduce_sum | solution.py:36
  78.2 1.4 %fusion.18 = f32[16,512]{1,0:T(8,128)S(1)} fusion(s32[2048]{0:T(1024)S(1)} %sub.44, f32[16,2048]{1,0:T(8,128)S(1)} %fusion.15, pred[2048]{0:T(1024)(128)(4,1)S(1)} %broadcast_compare_fusion), kind=kOutput, calls=%fused_computation.29 | convolution fusion | flops 202407936 | bytes 174080 | tf_op jit(solution)/shard_map/dot_general | solution.py:90
  79.7 1.0 %fusion.24 = f32[1024,16]{1,0:T(8,128)S(1)} fusion(f32[16,512]{1,0:T(8,128)S(1)} %fusion.18, s32[512]{0:T(512)S(1)} %convert_add_fusion.1), kind=kOutput, calls=%fused_computation.38 | convolution fusion | flops 101187584 | bytes 100352 | tf_op jit(solution)/shard_map/dot_general | solution.py:96
  80.9 9.4 %all_to_all.19 = f32[32,1,512]{2,1,0:T(1,128)S(1)} all-to-all(f32[32,1,512]{2,1,0:T(1,128)S(1)} %all_to_all.16), channel_id=1, replica_groups=mesh['grp'=4,'dev'=8] {'grp','dev'}, dimensions={0} | all-to-all | bytes 131072 | tf_op jit(solution)/shard_map/all_to_all | solution.py:98
  90.3 0.6 copy.54
  (27 shorter events, 1.7 us)
Async XLA Ops:
  0.0 52.9 %copy-start = (f32[64,16]{0,1:T(8,128)S(1)}, f32[64,16]{0,1:T(8,128)}, u32[]{:S(2)}) copy-start(f32[64,16]{0,1:T(8,128)} %param.16) | copy-start | bytes 12292
  0.0 20.9 %copy-start.1 = (f32[3,8192]{1,0:T(4,128)S(1)}, f32[3,8192]{1,0:T(4,128)}, u32[]{:S(2)}) copy-start(f32[3,8192]{1,0:T(4,128)} %param.14) | copy-start | bytes 294916
  0.0 21.1 %copy-start.2 = (f32[3,512]{1,0:T(4,128)S(1)}, f32[3,512]{1,0:T(4,128)}, u32[]{:S(2)}) copy-start(f32[3,512]{1,0:T(4,128)} %param.13) | copy-start | bytes 18436
  0.0 21.7 %copy-start.3 = (s32[512,1]{0,1:T(1,128)S(1)}, s32[512,1]{0,1:T(1,128)}, u32[]{:S(2)}) copy-start(s32[512,1]{0,1:T(1,128)} %param.15) | copy-start | bytes 6148
  13.4 34.9 %all-to-all-start = ((f32[65,32,64]{0,2,1:T(8,128)}), f32[65,32,64]{0,2,1:T(8,128)S(1)}, u32[]{:S(2)}, u32[]{:S(2)}) async-start(f32[65,32,64]{0,2,1:T(8,128)} %bitcast.5), calls=%async_computation | async-start | bytes 2097152 | tf_op jit(solution)/shard_map/all_to_all | solution.py:73
  52.9 11.1 %copy-start.4 = (f32[64]{0:T(128)S(1)}, f32[64]{0:T(128)}, u32[]{:S(2)}) copy-start(f32[64]{0:T(128)} %param.17) | copy-start | bytes 772
where the time goes:
time: 91.4 us; the launch traced here: 91 us
  waiting for transfers between devices  26.3 us (29%)
  other arithmetic  25.4 us (28%)
  matrix products  15.4 us (17%)
  blocking collectives  9.41 us (10%)
  starting transfers between devices  7.49 us (8%)
  local copies, waits for them, and re-layouts  6.79 us (7%)
    all_to_all x1, waiting for transfers between devices, per_device(): lax.all_to_all(outgoing, ('grp', 'dev'), split_axis=1, concat_axis=1, til...  26.3 us
    reduce_sum x1, other arithmetic, expansion_terms(): return jnp.sum(scale[:, None, :] * total, axis=0)  14.1 us
    all_to_all x1, blocking collectives, per_device(): lax.all_to_all(sending, ('grp', 'dev'), split_axis=0, concat_axis=0, tile...  9.41 us
    all_to_all x1, matrix products, per_device(): lax.all_to_all(outgoing, ('grp', 'dev'), split_axis=1, concat_axis=1, til...  7.97 us
    reduce_sum x1, other arithmetic, expansion_terms(): inner = jnp.sum(src[:, :, None, :] * rel_targets[:, None, :, :], axis=0)  7.67 us
    all_to_all x1, starting transfers between devices, per_device(): lax.all_to_all(outgoing, ('grp', 'dev'), split_axis=1, concat_axis=1, til...  7.49 us
    dot_general x1, matrix products, per_device(): lax.dot_general(centre_data, pick, (((1,), (1,)), ((), ())), precision=HI)  2.24 us
    dot_general x1, matrix products, per_device(): upper = jnp.einsum('jn,cns->cjs', upsample, coarse_in, precision=HI)  1.89 us
  transfers between devices with their start and end apart: 1, of which 1 were waited for; matrix products, arithmetic and copies ran while one was open for 1% of the time, Pallas kernels for 0%

commit v1 on v0

--- a/solution.py
+++ b/solution.py
@@ -70,7 +70,15 @@
     slot_index = destination * capacity + route_rank(destination, devices)
     place = (slot_index[:, None] == jnp.arange(slots, dtype=jnp.int32)[None, :]).astype(jnp.float32)
     outgoing = jnp.dot(payload, place, precision=HI)
-    incoming = lax.all_to_all(outgoing, ("grp", "dev"), split_axis=1, concat_axis=1, tiled=True)
+    incoming = jnp.concatenate(
+        lax.all_to_all(
+            jnp.stack(jnp.split(outgoing, lax.axis_size(("grp", "dev")), axis=1)),
+            ("grp", "dev"),
+            0,
+            0,
+        ),
+        axis=1,
+    )
     ids = jnp.round(incoming[4 * nodes]).astype(jnp.int32) - 1
     valid = ids >= 0
     pick = (ids[:, None] == jnp.arange(centre_count, dtype=jnp.int32)[None, :]).astype(jnp.float32)

time: 91.4 us -> 88.2 us (0.965)
  matrix products: 15.4 us -> 10.8 us
  local copies, waits for them, and re-layouts: 6.79 us -> 8.95 us
    all_to_all x1 -> x0, matrix products: 7.97 us -> none  [per_device(): lax.all_to_all(outgoing, ('grp', 'dev'), split_axis=1, concat_axis=1, til...]
    dot_general x0 -> x1, matrix products: none -> 3.42 us  [per_device(): outgoing = jnp.dot(payload, place, precision=HI)]
    unnamed x12 -> x51, local copies, waits for them, and re-layouts: 1.49 us -> 3.84 us
    another operation x0 -> x2, local copies, waits for them, and re-layouts: none -> 1.48 us  [per_device(): jnp.stack(jnp.split(outgoing, lax.axis_size(('grp', 'dev')), axis=1))]
where the time goes in v1:
time: 88.2 us; the launch traced here: 87.8 us
  waiting for transfers between devices  26.1 us (30%)
  other arithmetic  24.7 us (28%)
  matrix products  10.8 us (12%)
  blocking collectives  9.41 us (11%)
  local copies, waits for them, and re-layouts  8.95 us (10%)
  starting transfers between devices  7.48 us (8%)
    all_to_all x1, waiting for transfers between devices, per_device(): lax.all_to_all(jnp.stack(jnp.split(outgoing, lax.axis_size(('grp', 'dev')...  26.1 us
    reduce_sum x1, other arithmetic, expansion_terms(): return jnp.sum(scale[:, None, :] * total, axis=0)  14.1 us
    all_to_all x1, blocking collectives, per_device(): lax.all_to_all(sending, ('grp', 'dev'), split_axis=0, concat_axis=0, tile...  9.41 us
    reduce_sum x1, other arithmetic, expansion_terms(): inner = jnp.sum(src[:, :, None, :] * rel_targets[:, None, :, :], axis=0)  7.67 us
    all_to_all x1, starting transfers between devices, per_device(): lax.all_to_all(jnp.stack(jnp.split(outgoing, lax.axis_size(('grp', 'dev')...  7.48 us
    unnamed x51, local copies, waits for them, and re-layouts  3.84 us
    dot_general x1, matrix products, per_device(): outgoing = jnp.dot(payload, place, precision=HI)  3.42 us
    dot_general x1, matrix products, per_device(): lax.dot_general(centre_data, pick, (((1,), (1,)), ((), ())), precision=HI)  2.23 us
  transfers between devices with their start and end apart: 1, of which 1 were waited for; matrix products, arithmetic and copies ran while one was open for 1% of the time, Pallas kernels for 0%

profile of v1, /device:TPU:0, one launch (start us, length us, event | category | flops | bytes accessed | tf_op | source)
XLA Modules:
  0.0 87.8 jit_solution(3625277085427249034)
XLA Ops:
  0.0 0.9 copy.46
  1.0 0.5 fusion.26
  1.6 0.3 reshape.131
  1.9 0.2 copy.41
  3.3 3.4 %fusion.17 = f32[65,2048]{1,0:T(8,128)S(1)} fusion(s32[1024]{0:T(1024)S(1)} %convert_add_fusion, f32[1,1024]{0,1:T(8,128)S(1)} %convert_element_type.66, f32[64,1024]{0,1:T(8,128)S(1)} %bitcast.158), kind=kOutput, calls=%fused_computation.27 | convolution fusion | flops 1637942272 | bytes 802816 | tf_op jit(solution)/shard_map/dot_general | solution.py:72
  8.1 1.4 %copy.47 = f32[32,65,64]{1,2,0:T(8,128)} copy(f32[32,65,64]{2,1,0:T(8,128)S(1)} %constant_dynamic-update-slice_fusion) | data formatting | bytes 1064960 | tf_op jit(solution)/shard_map/stack | solution.py:75
  9.5 7.5 %all-to-all-start = ((f32[32,65,64]{1,2,0:T(8,128)}), f32[32,65,64]{1,2,0:T(8,128)S(1)}, u32[]{:S(2)}, u32[]{:S(2)}) async-start(f32[32,65,64]{1,2,0:T(8,128)} %copy.47), calls=%async_computation | async-start | bytes 2097152 | tf_op jit(solution)/shard_map/all_to_all | solution.py:74
  17.0 0.3 reshape.138
  17.3 0.3 subtract_bitcast_fusion
  18.0 0.3 fusion.27
  18.3 26.1 %all-to-all-done = f32[32,65,64]{1,2,0:T(8,128)S(1)} async-done(((f32[32,65,64]{1,2,0:T(8,128)}), f32[32,65,64]{1,2,0:T(8,128)S(1)}, u32[]{:S(2)}, u32[]{:S(2)}) %all-to-all-start) | async-done | bytes 532512 | tf_op jit(solution)/shard_map/all_to_all | solution.py:74
  44.4 0.9 %fusion.30 = s32[32,64]{1,0:T(8,128)S(1)} fusion(f32[65,32,64]{0,2,1:T(8,128)S(1)} %bitcast.153), kind=kLoop, calls=%fused_computation.48 | loop fusion | flops 6144 | bytes 16384 | tf_op jit(solution)/shard_map/sub | solution.py:82
  45.4 2.2 %fusion.19 = f32[51,2048]{1,0:T(8,128)S(1)} fusion(s32[2048]{0:T(1024)S(1)} %sub.44, f32[48,512]{1,0:T(8,128)S(1)} %bitcast.162, f32[3,512]{1,0:T(4,128)S(1)} %copy-done.5), kind=kOutput, calls=%fused_computation.30 | convolution fusion | flops 642803200 | bytes 530432 | tf_op jit(solution)/shard_map/dot_general | solution.py:90
  47.7 0.7 copy-done.1
  48.4 0.9 %copy.48 = f32[64,32,64]{2,1,0:T(8,128)S(1)} copy(f32[64,32,64]{0,2,1:T(8,128)S(1)} %bitcast.154) | data formatting | bytes 1048576 | tf_op jit(solution)/shard_map/slice | solution.py:93
  49.3 0.4 reshape.137
  49.7 1.9 %convolution_bitcast_fusion = f32[4,64,2048]{2,1,0:T(8,128)S(1)} fusion(f32[4,16,2048]{2,1,0:T(8,128)S(1)} %reshape.137, f32[64,16]{0,1:T(8,128)S(1)} %copy-done), kind=kOutput, calls=%fused_computation.34 | convolution fusion | flops 100663296 | bytes 2625536 | tf_op jit(solution)/shard_map/jn,cns->cjs/dot_general | solution.py:94
  51.6 1.5 %multiply_reduce_fusion.1 = (f32[64,2048]{1,0:T(8,128)S(1)}, f32[3,64,2048]{2,1,0:T(8,128)}) fusion(f32[3,2048]{1,0:T(4,128)S(1)} %slice-done, f32[4,64,2048]{2,1,0:T(8,128)S(1)} %convolution_bitcast_fusion), kind=kLoop, calls=%fused_computation.40 | loop fusion | flops 1048576 | bytes 3694592 | tf_op jit(solution)/shard_map/reduce_sum | solution.py:22
  53.1 7.7 %multiply_reduce_fusion = f32[64,16,2048]{2,1,0:T(8,128)} fusion(f32[3,16,2048]{2,1,0:T(8,128)S(1)} %bitcast.156, f32[3,64,2048]{2,1,0:T(8,128)} %get-tuple-element.6), kind=kLoop, calls=%fused_computation.7 | loop fusion | flops 10485760 | bytes 10354688 | tf_op jit(solution)/shard_map/reduce_sum | solution.py:26
  61.0 14.1 %fusion.15 = f32[16,2048]{1,0:T(8,128)S(1)} fusion(f32[64,16,2048]{2,1,0:T(8,128)} %multiply_reduce_fusion, f32[16,2048]{1,0:T(8,128)S(1)} %multiply_reduce_fusion.2, f32[64,2048]{1,0:T(8,128)S(1)} %get-tuple-element.8, f32[64,2048]{1,0:T(8,128)S(1)} %get-tuple-element.7), kind=kLoop, calls=%fused_computation.24 | loop fusion | flops 96436224 | bytes 9699328 | tf_op jit(solution)/shard_map/reduce_sum | solution.py:36
  75.1 1.4 %fusion.18 = f32[16,512]{1,0:T(8,128)S(1)} fusion(s32[2048]{0:T(1024)S(1)} %sub.44, f32[16,2048]{1,0:T(8,128)S(1)} %fusion.15, pred[2048]{0:T(1024)(128)(4,1)S(1)} %broadcast_compare_fusion), kind=kOutput, calls=%fused_computation.29 | convolution fusion | flops 202407936 | bytes 174080 | tf_op jit(solution)/shard_map/dot_general | solution.py:98
  76.5 1.0 %fusion.24 = f32[1024,16]{1,0:T(8,128)S(1)} fusion(f32[16,512]{1,0:T(8,128)S(1)} %fusion.18, s32[512]{0:T(512)S(1)} %convert_add_fusion.1), kind=kOutput, calls=%fused_computation.38 | convolution fusion | flops 101187584 | bytes 100352 | tf_op jit(solution)/shard_map/dot_general | solution.py:104
  77.8 9.4 %all_to_all.15 = f32[32,1,512]{2,1,0:T(1,128)S(1)} all-to-all(f32[32,1,512]{2,1,0:T(1,128)S(1)} %all_to_all.12), channel_id=1, replica_groups=mesh['grp'=4,'dev'=8] {'grp','dev'}, dimensions={0} | all-to-all | bytes 131072 | tf_op jit(solution)/shard_map/all_to_all | solution.py:106
  87.2 0.6 copy.85
  (69 shorter events, 3.5 us)
Async XLA Ops:
  0.0 49.7 %copy-start = (f32[64,16]{0,1:T(8,128)S(1)}, f32[64,16]{0,1:T(8,128)}, u32[]{:S(2)}) copy-start(f32[64,16]{0,1:T(8,128)} %param.16) | copy-start | bytes 12292
  0.0 1.6 %copy-start.2 = (f32[3,8192]{1,0:T(4,128)S(1)}, f32[3,8192]{1,0:T(4,128)}, u32[]{:S(2)}) copy-start(f32[3,8192]{1,0:T(4,128)} %param.9) | copy-start | bytes 294916
  1.6 0.8 copy-start.4
  1.9 0.8 copy-start.6
  9.5 7.5 %copy-start.3 = (f32[3,8192]{1,0:T(4,128)S(1)}, f32[3,8192]{1,0:T(4,128)}, u32[]{:S(2)}) copy-start(f32[3,8192]{1,0:T(4,128)} %param.14) | copy-start | bytes 294916
  9.5 7.8 %copy-start.5 = (f32[3,512]{1,0:T(4,128)S(1)}, f32[3,512]{1,0:T(4,128)}, u32[]{:S(2)}) copy-start(f32[3,512]{1,0:T(4,128)} %param.13) | copy-start | bytes 18436
  9.5 34.9 %all-to-all-start = ((f32[32,65,64]{1,2,0:T(8,128)}), f32[32,65,64]{1,2,0:T(8,128)S(1)}, u32[]{:S(2)}, u32[]{:S(2)}) async-start(f32[32,65,64]{1,2,0:T(8,128)} %copy.47), calls=%async_computation | async-start | bytes 2097152 | tf_op jit(solution)/shard_map/all_to_all | solution.py:74
  17.3 0.7 copy-start.7
  47.6 0.8 copy-start.1
  49.7 1.9 %slice-start = ((f32[51,2048]{1,0:T(8,128)}), f32[3,2048]{1,0:T(4,128)S(1)}, s32[]{:S(2)}) async-start(f32[51,2048]{1,0:T(8,128)} %copy-done.1), calls=%async_computation.2 | async-start | bytes 65536 | tf_op jit(solution)/shard_map/slice | solution.py:91
  53.1 7.7 %copy-start.8 = (f32[64]{0:T(128)S(1)}, f32[64]{0:T(128)}, u32[]{:S(2)}) copy-start(f32[64]{0:T(128)} %param.17) | copy-start | bytes 772
